TPU v7x, 32 devices: a whole 2x2x4 slice. The times are simulated.
32 devices in a mesh: rep: 2 (over y), seq: 4 (over z), head: 4 (over x, core).
Axes of the slice: x: 2, y: 2, z: 4, core: 2. Of those that a mesh axis runs over, the one named last changes fastest.
Arguments:
- queries: bfloat16 [3072, 2560], P(('rep', 'seq'), 'head'), parts along dimension 0, may hold values from -16 to 16
- keys: bfloat16 [3072, 2560], P(('rep', 'seq'), 'head'), parts along dimension 0, may hold values from -6 to 6
- values: bfloat16 [3072, 2560], P(('rep', 'seq'), 'head'), parts along dimension 0, may hold values from -6 to 6
- out_weight: bfloat16 [2560, 5120], P('seq', 'head'), may hold values from -0.3125 to 0.3125
- neighbours: int32 [8, 27], P('rep'), parts along dimension 0, may hold values from -1 to 3, as said below
- clip_ids: int32 [3072], P(('rep', 'seq')), parts along dimension 0, may hold values from 0 to 1
Outputs:
- output: bfloat16 [3072, 5120], P(('rep', 'seq'), 'head'), parts along dimension 0
There are 2 independent parts, one for each index of `rep`. A program takes and returns all parts, laid end to end along the dimension named above; an argument that names none is the same for every part. Nothing has to cross between parts.
Inputs may be any that keep to these rules, and one draw needn't show every extreme that they name: `neighbours`: column 9 (a + 1) + 3 (b + 1) + (c + 1) of row s, for a, b, c each -1, 0 or 1, is either -1 or s + a * 4 * 7 + b * 7 + c; column 13 of row s is s.
All inputs are finite; a program needn't handle non-finite values.
Results may differ from a plain program's by a relative error of at most 0.0058.
Values may be sent and summed in bfloat16 or wider, within the bound.
No kernel may reach another device: no remote copies, remote signals or barrier semaphores. Data moves between devices by JAX's collectives and lax.ppermute only.
A program may use at most 192 MiB of HBM per device.

v0:
```python
import math
import jax
import jax.numpy as jnp
from jax import lax
from jax.sharding import PartitionSpec as P

HD = 128
TGH = 4
TGW = 7


def from_behind(value, axis, by):
    peers = lax.axis_size(axis)
    pairs = [(i, i + by) for i in range(peers) if 0 <= i + by < peers]
    return lax.ppermute(value, axis, pairs)


def attend_head(query_head, key_head, value_head, allowed):
    scores = lax.dot_general(
        query_head, key_head, (((1,), (1,)), ((), ())), preferred_element_type=jnp.float32
    ) * (1.0 / math.sqrt(query_head.shape[1]))
    masked = jnp.where(allowed, scores, -1e30)
    highest = jnp.max(masked, axis=1, keepdims=True)
    raised = jnp.where(allowed, jnp.exp(masked - highest), 0.0)
    summed = jnp.sum(raised, axis=1, keepdims=True)
    weights = (raised / summed).astype(jnp.bfloat16)
    return jnp.dot(weights, value_head, preferred_element_type=jnp.float32).astype(jnp.bfloat16)


def on_device(queries, keys, values, out_weight, neighbours, clip_ids):
    tile_rows = queries.shape[0]
    feature_width = queries.shape[1]
    seq_count = lax.axis_size("seq")
    layer_tiles = TGH * TGW
    every_offset = set()
    for layer_step in (-1, 0, 1):
        for row_step in (-1, 0, 1):
            for col_step in (-1, 0, 1):
                every_offset.add(layer_step * layer_tiles + row_step * TGW + col_step)
    distances = [offset for offset in sorted(every_offset) if 0 < offset < seq_count]
    key_list = [keys]
    value_list = [values]
    clip_list = [clip_ids]
    offsets = [0]
    for distance in distances:
        below_keys, below_values, below_clips = from_behind(
            (keys, values, clip_ids), "seq", distance
        )
        above_keys, above_values, above_clips = from_behind(
            (keys, values, clip_ids), "seq", -distance
        )
        key_list += [below_keys, above_keys]
        value_list += [below_values, above_values]
        clip_list += [below_clips, above_clips]
        offsets += [distance, -distance]
    key_stack = jnp.stack(key_list)
    value_stack = jnp.stack(value_list)
    clip_stack = jnp.stack(clip_list)
    blocks = key_stack.shape[0]
    position = lax.axis_index("seq")
    window_row = lax.dynamic_index_in_dim(neighbours, position, 0, keepdims=False)
    sources = position - jnp.asarray(offsets, dtype=jnp.int32)
    present = jnp.any(
        (window_row[None, :] == sources[:, None]) & (window_row[None, :] >= 0), axis=1
    )
    key_clips = clip_stack.reshape(blocks * tile_rows)
    allowed = jnp.repeat(present, tile_rows)[None, :] & (clip_ids[:, None] == key_clips[None, :])
    key_rows = key_stack.reshape(blocks * tile_rows, feature_width)
    value_rows = value_stack.reshape(blocks * tile_rows, feature_width)
    head_outputs = []
    for head_index in range(feature_width // HD):
        first_col = head_index * HD
        head_outputs.append(
            attend_head(
                queries[:, first_col : first_col + HD],
                key_rows[:, first_col : first_col + HD],
                value_rows[:, first_col : first_col + HD],
                allowed,
            )
        )
    attended = jnp.concatenate(head_outputs, axis=1)
    all_features = lax.all_gather(attended, "head", axis=1, tiled=True)
    empty = jnp.zeros((tile_rows, out_weight.shape[1]), jnp.float32)
    weight_piece = lax.all_gather(out_weight, "seq", axis=0, tiled=True)
    features = lax.slice_in_dim(all_features, 0, weight_piece.shape[0], axis=1)
    projected = empty + jnp.dot(features, weight_piece, preferred_element_type=jnp.float32)
    return projected.astype(jnp.bfloat16)


def solution(mesh):
    in_specs = (
        P(("rep", "seq"), "head"),
        P(("rep", "seq"), "head"),
        P(("rep", "seq"), "head"),
        P("seq", "head"),
        P("rep", None),
        P(("rep", "seq")),
    )
    out_specs = P(("rep", "seq"), "head")
    return jax.shard_map(
        on_device, mesh=mesh, in_specs=in_specs, out_specs=out_specs, check_vma=False
    )
```

profile of v0, /device:TPU:0, one launch (start us, length us, event | category | flops | bytes accessed | tf_op | source)
XLA Modules:
  0.0 208.0 jit_solution(14518805611755408136)
XLA Ops:
  6.5 5.0 %collective-permute-start = (s32[384]{0:T(512)}, s32[384]{0:T(512)S(1)}, u32[]{:S(2)}, u32[]{:S(2)}) collective-permute-start(s32[384]{0:T(512)} %param.12), channel_id=1, source_target_pairs={{0,4},{4,8},{8,12},{1,5},{5,9},{9,13},{2,6},{6,10},{10,14},{3,7},{... | collective-permute-start | bytes 4616 | tf_op jit(solution)/shard_map/ppermute | solution.py:15
  11.6 1.3 collective-permute-start.1
  12.9 4.6 %collective-permute-start.2 = (bf16[384,640]{1,0:T(8,128)(2,1)}, bf16[384,640]{1,0:T(8,128)(2,1)S(1)}, u32[]{:S(2)}, u32[]{:S(2)}) collective-permute-start(bf16[384,640]{1,0:T(8,128)(2,1)} %param.8), channel_id=1, source_target_pairs={{0,4},{4,8},{8,12},{1,5},{5,9},{9,13},{2,6},{6,10},{10,14},{3,7},{... | collective-permute-start | bytes 1474568 | tf_op jit(solution)/shard_map/ppermute | solution.py:15
  17.5 1.3 collective-permute-start.3
  18.8 4.6 %collective-permute-start.4 = (bf16[384,640]{1,0:T(8,128)(2,1)}, bf16[384,640]{1,0:T(8,128)(2,1)S(1)}, u32[]{:S(2)}, u32[]{:S(2)}) collective-permute-start(bf16[384,640]{1,0:T(8,128)(2,1)} %param.9), channel_id=1, source_target_pairs={{0,4},{4,8},{8,12},{1,5},{5,9},{9,13},{2,6},{6,10},{10,14},{3,7},{... | collective-permute-start | bytes 1474568 | tf_op jit(solution)/shard_map/ppermute | solution.py:15
  23.4 0.7 compare_bitcast_fusion
  24.1 0.7 fusion.35
  24.8 0.7 broadcast_add_fusion
  25.4 0.2 and_reduce_fusion
  25.6 0.7 stack.36
  26.4 1.3 collective-permute-start.5
  27.8 1.7 collective-permute-done.2
  29.4 4.3 %collective-permute-done.3 = bf16[384,640]{1,0:T(8,128)(2,1)S(1)} collective-permute-done((bf16[384,640]{1,0:T(8,128)(2,1)}, bf16[384,640]{1,0:T(8,128)(2,1)S(1)}, u32[]{:S(2)}, u32[]{:S(2)}) %collective-permute-start.3) | collective-permute-done | bytes 491552 | tf_op jit(solution)/shard_map/ppermute | solution.py:15
  33.8 1.2 pad_maximum_fusion
  35.0 0.6 fusion.41
  35.6 0.6 fusion.42
  36.3 0.6 fusion.43
  36.9 0.6 fusion.44
  37.5 0.6 fusion.45
  38.2 4.0 %collective-permute-done.5 = bf16[384,640]{1,0:T(8,128)(2,1)S(1)} collective-permute-done((bf16[384,640]{1,0:T(8,128)(2,1)}, bf16[384,640]{1,0:T(8,128)(2,1)S(1)}, u32[]{:S(2)}, u32[]{:S(2)}) %collective-permute-start.5) | collective-permute-done | bytes 491552 | tf_op jit(solution)/shard_map/ppermute | solution.py:15
  42.3 0.2 pad_maximum_fusion.1
  42.4 2.3 %fusion.14 = (f32[384]{0:T(512)S(1)}, f32[384]{0:T(512)S(1)}, f32[384]{0:T(512)S(1)}, f32[384]{0:T(512)S(1)}, f32[384]{0:T(512)S(1)}) fusion(f32[384,1152]{0,1:T(8,128)S(1)} %get-tuple-element.11, f32[384]{0:T(512)S(1)} %get-tuple-element.10, s32[384]{0:T(512)S(1)} %copy-done.2, s32[1152]{0:T(1024)S(1)} %eq.35, pred[1152]{0:T(1024)(128)(4,1)S(1)} %and.24, ...), kind=kLoop, calls=%fused_computation.33 | loop fusion | flops 7518336 | bytes 8870016 | tf_op jit(solution)/shard_map/reduce_sum | solution.py:25
  44.7 1.0 fusion.15
  45.7 1.0 fusion.16
  46.8 1.0 fusion.17
  47.8 1.0 fusion.18
  48.8 1.0 fusion.19
  49.8 0.8 copy-done.1
  50.7 0.7 all-gather.5.cloned.1.call-update
  51.4 21.5 %all-gather.3.cloned.1.call-done = bf16[384,2560]{1,0:T(8,128)(2,1)} async-done(((bf16[384,640]{1,0:T(8,128)(2,1)}), bf16[384,2560]{1,0:T(8,128)(2,1)}) %all-gather.3.cloned.1.call-update) | async-done | bytes 1966096 | tf_op jit(solution)/shard_map/all_gather | solution.py:82
  72.8 121.2 %all-gather.5.cloned.1.call-done = bf16[2560,1280]{1,0:T(8,128)(2,1)} async-done(((bf16[640,1280]{1,0:T(8,128)(2,1)}), bf16[2560,1280]{1,0:T(8,128)(2,1)}) %all-gather.5.cloned.1.call-update) | async-done | bytes 6553616 | tf_op jit(solution)/shard_map/all_gather | solution.py:84
  194.1 7.1 %convolution_convert_fusion = bf16[384,1280]{1,0:T(8,128)(2,1)} fusion(bf16[384,2560]{1,0:T(8,128)(2,1)} %all-gather.3.cloned.1.call-done, bf16[2560,1280]{1,0:T(8,128)(2,1)} %all-gather.5.cloned.1.call-done), kind=kOutput, calls=%fused_computation.15 | convolution fusion | flops 2517073920 | bytes 9502720 | tf_op jit(solution)/shard_map/dot_general | solution.py:86
  (19 shorter events, 0.3 us)
Async XLA Ops:
  6.5 28.4 %copy-start.2 = (s32[384]{0:T(512)S(1)}, s32[384]{0:T(512)}, u32[]{:S(2)}) copy-start(s32[384]{0:T(512)} %param.12) | copy-start | bytes 4612
  6.5 28.5 %copy-start.3 = (bf16[384,640]{1,0:T(8,128)(2,1)S(1)}, bf16[384,640]{1,0:T(8,128)(2,1)}, u32[]{:S(2)}) copy-start(bf16[384,640]{1,0:T(8,128)(2,1)} %param.7) | copy-start | bytes 1474564
  6.5 66.3 %all-gather.3.cloned.1.call-start = ((), (), s32[]{:S(2)}) async-start(), calls=%async_computation | async-start | bytes 2457600 | tf_op jit(solution)/shard_map/all_gather | solution.py:82
  6.5 19.8 %collective-permute-start = (s32[384]{0:T(512)}, s32[384]{0:T(512)S(1)}, u32[]{:S(2)}, u32[]{:S(2)}) collective-permute-start(s32[384]{0:T(512)} %param.12), channel_id=1, source_target_pairs={{0,4},{4,8},{8,12},{1,5},{5,9},{9,13},{2,6},{6,10},{10,14},{3,7},{... | collective-permute-start | bytes 4616 | tf_op jit(solution)/shard_map/ppermute | solution.py:15
  11.6 16.1 %collective-permute-start.1 = (s32[384]{0:T(512)}, s32[384]{0:T(512)S(1)}, u32[]{:S(2)}, u32[]{:S(2)}) collective-permute-start(s32[384]{0:T(512)} %param.12), channel_id=1, source_target_pairs={{4,0},{8,4},{12,8},{5,1},{9,5},{13,9},{6,2},{10,6},{14,10},{7,3},{... | collective-permute-start | bytes 4616 | tf_op jit(solution)/shard_map/ppermute | solution.py:15
  12.9 16.5 %collective-permute-start.2 = (bf16[384,640]{1,0:T(8,128)(2,1)}, bf16[384,640]{1,0:T(8,128)(2,1)S(1)}, u32[]{:S(2)}, u32[]{:S(2)}) collective-permute-start(bf16[384,640]{1,0:T(8,128)(2,1)} %param.8), channel_id=1, source_target_pairs={{0,4},{4,8},{8,12},{1,5},{5,9},{9,13},{2,6},{6,10},{10,14},{3,7},{... | collective-permute-start | bytes 1474568 | tf_op jit(solution)/shard_map/ppermute | solution.py:15
  17.5 16.3 %collective-permute-start.3 = (bf16[384,640]{1,0:T(8,128)(2,1)}, bf16[384,640]{1,0:T(8,128)(2,1)S(1)}, u32[]{:S(2)}, u32[]{:S(2)}) collective-permute-start(bf16[384,640]{1,0:T(8,128)(2,1)} %param.8), channel_id=1, source_target_pairs={{4,0},{8,4},{12,8},{5,1},{9,5},{13,9},{6,2},{10,6},{14,10},{7,3},{... | collective-permute-start | bytes 1474568 | tf_op jit(solution)/shard_map/ppermute | solution.py:15
  18.8 19.4 %collective-permute-start.4 = (bf16[384,640]{1,0:T(8,128)(2,1)}, bf16[384,640]{1,0:T(8,128)(2,1)S(1)}, u32[]{:S(2)}, u32[]{:S(2)}) collective-permute-start(bf16[384,640]{1,0:T(8,128)(2,1)} %param.9), channel_id=1, source_target_pairs={{0,4},{4,8},{8,12},{1,5},{5,9},{9,13},{2,6},{6,10},{10,14},{3,7},{... | collective-permute-start | bytes 1474568 | tf_op jit(solution)/shard_map/ppermute | solution.py:15
  26.4 15.9 %collective-permute-start.5 = (bf16[384,640]{1,0:T(8,128)(2,1)}, bf16[384,640]{1,0:T(8,128)(2,1)S(1)}, u32[]{:S(2)}, u32[]{:S(2)}) collective-permute-start(bf16[384,640]{1,0:T(8,128)(2,1)} %param.9), channel_id=1, source_target_pairs={{4,0},{8,4},{12,8},{5,1},{9,5},{13,9},{6,2},{10,6},{14,10},{7,3},{... | collective-permute-start | bytes 1474568 | tf_op jit(solution)/shard_map/ppermute | solution.py:15
  37.5 4.7 %copy-start = (bf16[384,640]{1,0:T(8,128)(2,1)S(1)}, bf16[384,640]{1,0:T(8,128)(2,1)}, u32[]{:S(2)}) copy-start(bf16[384,640]{1,0:T(8,128)(2,1)} %param.9) | copy-start | bytes 1474564
  49.8 0.8 copy-start.1
  50.6 143.4 %all-gather.5.cloned.1.call-start = ((), (), s32[]{:S(2)}) async-start(), calls=%async_computation.1 | async-start | bytes 8192000 | tf_op jit(solution)/shard_map/all_gather | solution.py:84
Sparse Core Ops, SparseCore 0:
  50.7 22.0 all-gather.2
  74.4 119.6 all-gather.4
where the time goes:
time: 208 us
  waiting for transfers between devices  154 us (74%)
  starting transfers between devices  18.1 us (9%)
  matrix products  15.3 us (7%)
  between operations  13.6 us (7%)
  other arithmetic  5.25 us (3%)
  local copies, waits for them, and re-layouts  2.27 us (1%)
    all_gather x1, waiting for transfers between devices, on_device(): weight_piece = lax.all_gather(out_weight, 'seq', axis=0, tiled=True)  121 us
    all_gather x1, waiting for transfers between devices, on_device(): all_features = lax.all_gather(attended, 'head', axis=1, tiled=True)  21.5 us
    ppermute x6, starting transfers between devices, from_behind(): return lax.ppermute(value, axis, pairs)  18.1 us
    ppermute x6, waiting for transfers between devices, from_behind(): return lax.ppermute(value, axis, pairs)  10.1 us
    dot_general x1, matrix products, on_device(): jnp.dot(features, weight_piece, preferred_element_type=jnp.float32)  7.1 us
    dot_general x5, matrix products, attend_head(): jnp.dot(weights, value_head, preferred_element_type=jnp.float32)  5.04 us
  transfers between devices with their start and end apart: 8, of which 6 were waited for; matrix products, arithmetic and copies ran while one was open for 4% of the time, Pallas kernels for 0%

commit v1 on v0

--- a/solution.py
+++ b/solution.py
@@ -7,6 +7,24 @@
 HD = 128
 TGH = 4
 TGW = 7
+
+
+def collect(shard, axis, dim):
+    ways, here, step = (lax.axis_size(axis), lax.axis_index(axis), shard.shape[dim])
+    dims = [n * ways if d == dim else n for d, n in enumerate(shard.shape)]
+    full = lax.dynamic_update_slice_in_dim(
+        jnp.zeros(dims, shard.dtype), shard, here * step, axis=dim
+    )
+    going_up = going_down = shard
+    for far in range(1, ways // 2 + 1):
+        going_up = lax.ppermute(going_up, axis, [(d, (d + 1) % ways) for d in range(ways)])
+        full = lax.dynamic_update_slice_in_dim(full, going_up, (here - far) % ways * step, axis=dim)
+        if 2 * far < ways:
+            going_down = lax.ppermute(going_down, axis, [(d, (d - 1) % ways) for d in range(ways)])
+            full = lax.dynamic_update_slice_in_dim(
+                full, going_down, (here + far) % ways * step, axis=dim
+            )
+    return full
 
 
 def from_behind(value, axis, by):
@@ -81,7 +99,7 @@
     attended = jnp.concatenate(head_outputs, axis=1)
     all_features = lax.all_gather(attended, "head", axis=1, tiled=True)
     empty = jnp.zeros((tile_rows, out_weight.shape[1]), jnp.float32)
-    weight_piece = lax.all_gather(out_weight, "seq", axis=0, tiled=True)
+    weight_piece = collect(out_weight, "seq", 0)
     features = lax.slice_in_dim(all_features, 0, weight_piece.shape[0], axis=1)
     projected = empty + jnp.dot(features, weight_piece, preferred_element_type=jnp.float32)
     return projected.astype(jnp.bfloat16)

time: 208 us -> 167 us (0.80)
  waiting for transfers between devices: 154 us -> 91 us
  local copies, waits for them, and re-layouts: 2.27 us -> 12.7 us
  starting transfers between devices: 18.1 us -> 24.4 us
  matrix products: 15.3 us -> 18.5 us
    all_gather x1 -> x0, waiting for transfers between devices: 121 us -> none  [on_device(): weight_piece = lax.all_gather(out_weight, 'seq', axis=0, tiled=True)]
    ppermute x0 -> x3, waiting for transfers between devices: none -> 83.5 us  [the longest x2 54.1 us: collect(): lax.ppermute(going_up, axis, [(d, (d + 1) % ways) for d in range(ways)])]
    all_gather x1, waiting for transfers between devices: 21.5 us -> 0.01 us  [on_device(): all_features = lax.all_gather(attended, 'head', axis=1, tiled=True)]
    dynamic_update_slice x0 -> x4, local copies, waits for them, and re-layouts: none -> 8.02 us  [the longest x2 4.01 us: collect(): lax.dynamic_update_slice_in_dim(full, going_up, (here - far) % ways * ste...]
    ppermute x0 -> x3, starting transfers between devices: none -> 6.3 us  [the longest x1 3.6 us: collect(): lax.ppermute(going_down, axis, [(d, (d - 1) % ways) for d in range(ways)])]
    dot_general x5, matrix products: 5.04 us -> 8.21 us  [attend_head(): jnp.dot(weights, value_head, preferred_element_type=jnp.float32)]
    broadcast_in_dim x0 -> x1, local copies, waits for them, and re-layouts: none -> 3.16 us  [collect(): jnp.zeros(dims, shard.dtype)]
    ppermute x6, waiting for transfers between devices: 10.1 us -> 7.52 us  [from_behind(): return lax.ppermute(value, axis, pairs)]
  transfers between devices with their start and end apart: 8 -> 10, of which waited for: 6 -> 6; matrix products, arithmetic and copies ran while one was open for 4% -> 18% of each run, Pallas kernels for 0% -> 0%
where the time goes in v1:
time: 167 us; the launch traced here: 166 us
  waiting for transfers between devices  91 us (54%)
  starting transfers between devices  24.4 us (15%)
  matrix products  18.5 us (11%)
  between operations  13.5 us (8%)
  local copies, waits for them, and re-layouts  12.7 us (8%)
  other arithmetic  6.31 us (4%)
    ppermute x2, waiting for transfers between devices, collect(): lax.ppermute(going_up, axis, [(d, (d + 1) % ways) for d in range(ways)])  54.1 us
    ppermute x1, waiting for transfers between devices, collect(): lax.ppermute(going_down, axis, [(d, (d - 1) % ways) for d in range(ways)])  29.4 us
    ppermute x6, starting transfers between devices, from_behind(): return lax.ppermute(value, axis, pairs)  18.1 us
    dot_general x5, matrix products, attend_head(): jnp.dot(weights, value_head, preferred_element_type=jnp.float32)  8.21 us
    ppermute x6, waiting for transfers between devices, from_behind(): return lax.ppermute(value, axis, pairs)  7.52 us
    dot_general x1, matrix products, on_device(): jnp.dot(features, weight_piece, preferred_element_type=jnp.float32)  7.1 us
    dynamic_update_slice x2, local copies, waits for them, and re-layouts, collect(): lax.dynamic_update_slice_in_dim(full, going_up, (here - far) % ways * ste...  4.01 us
    ppermute x1, starting transfers between devices, collect(): lax.ppermute(going_down, axis, [(d, (d - 1) % ways) for d in range(ways)])  3.6 us
  transfers between devices with their start and end apart: 10, of which 6 were waited for; matrix products, arithmetic and copies ran while one was open for 18% of the time, Pallas kernels for 0%

profile of v1, /device:TPU:0, one launch (start us, length us, event | category | flops | bytes accessed | tf_op | source)
XLA Modules:
  0.0 166.4 jit_solution(18132266874616502192)
XLA Ops:
  6.5 5.0 %collective-permute-start = (s32[384]{0:T(512)}, s32[384]{0:T(512)S(1)}, u32[]{:S(2)}, u32[]{:S(2)}) collective-permute-start(s32[384]{0:T(512)} %param.12), channel_id=1, source_target_pairs={{0,4},{4,8},{8,12},{1,5},{5,9},{9,13},{2,6},{6,10},{10,14},{3,7},{... | collective-permute-start | bytes 4616 | tf_op jit(solution)/shard_map/ppermute | solution.py:33
  11.6 1.3 collective-permute-start.1
  12.9 4.6 %collective-permute-start.2 = (bf16[384,640]{1,0:T(8,128)(2,1)}, bf16[384,640]{1,0:T(8,128)(2,1)S(1)}, u32[]{:S(2)}, u32[]{:S(2)}) collective-permute-start(bf16[384,640]{1,0:T(8,128)(2,1)} %param.8), channel_id=1, source_target_pairs={{0,4},{4,8},{8,12},{1,5},{5,9},{9,13},{2,6},{6,10},{10,14},{3,7},{... | collective-permute-start | bytes 1474568 | tf_op jit(solution)/shard_map/ppermute | solution.py:33
  17.5 1.3 collective-permute-start.3
  18.8 4.6 %collective-permute-start.4 = (bf16[384,640]{1,0:T(8,128)(2,1)}, bf16[384,640]{1,0:T(8,128)(2,1)S(1)}, u32[]{:S(2)}, u32[]{:S(2)}) collective-permute-start(bf16[384,640]{1,0:T(8,128)(2,1)} %param.9), channel_id=1, source_target_pairs={{0,4},{4,8},{8,12},{1,5},{5,9},{9,13},{2,6},{6,10},{10,14},{3,7},{... | collective-permute-start | bytes 1474568 | tf_op jit(solution)/shard_map/ppermute | solution.py:33
  23.4 0.7 compare_bitcast_fusion
  24.1 0.7 fusion.35
  24.8 0.7 broadcast_add_fusion
  25.6 0.7 stack.36
  26.4 1.3 collective-permute-start.5
  27.7 2.7 %collective-permute-start.6 = (bf16[640,1280]{1,0:T(8,128)(2,1)}, bf16[640,1280]{1,0:T(8,128)(2,1)S(1)}, u32[]{:S(2)}, u32[]{:S(2)}) collective-permute-start(bf16[640,1280]{1,0:T(8,128)(2,1)} %param.10), channel_id=1, source_target_pairs={{0,4},{4,8},{8,12},{12,0},{1,5},{5,9},{9,13},{13,1},{2,6},{6,10},{... | collective-permute-start | bytes 4915208 | tf_op jit(solution)/shard_map/ppermute | solution.py:20
  30.5 3.3 %collective-permute-done.3 = bf16[384,640]{1,0:T(8,128)(2,1)S(1)} collective-permute-done((bf16[384,640]{1,0:T(8,128)(2,1)}, bf16[384,640]{1,0:T(8,128)(2,1)S(1)}, u32[]{:S(2)}, u32[]{:S(2)}) %collective-permute-start.3) | collective-permute-done | bytes 491552 | tf_op jit(solution)/shard_map/ppermute | solution.py:33
  33.8 1.2 pad_maximum_fusion
  38.2 1.8 %collective-permute-done.4 = bf16[384,640]{1,0:T(8,128)(2,1)S(1)} collective-permute-done((bf16[384,640]{1,0:T(8,128)(2,1)}, bf16[384,640]{1,0:T(8,128)(2,1)S(1)}, u32[]{:S(2)}, u32[]{:S(2)}) %collective-permute-start.4) | collective-permute-done | bytes 491552 | tf_op jit(solution)/shard_map/ppermute | solution.py:33
  40.0 2.4 %collective-permute-done.5 = bf16[384,640]{1,0:T(8,128)(2,1)} collective-permute-done((bf16[384,640]{1,0:T(8,128)(2,1)}, bf16[384,640]{1,0:T(8,128)(2,1)}, u32[]{:S(2)}, u32[]{:S(2)}) %collective-permute-start.5) | collective-permute-done | bytes 491552 | tf_op jit(solution)/shard_map/ppermute | solution.py:33
  42.4 1.2 pad_maximum_fusion.1
  43.6 2.3 %fusion.14 = (f32[384]{0:T(512)S(1)}, f32[384]{0:T(512)S(1)}, f32[384]{0:T(512)S(1)}, f32[384]{0:T(512)S(1)}, f32[384]{0:T(512)S(1)}) fusion(f32[384,1152]{0,1:T(8,128)S(1)} %get-tuple-element.11, f32[384]{0:T(512)S(1)} %get-tuple-element.10, s32[384]{0:T(512)S(1)} %copy-done.2, s32[1152]{0:T(1024)S(1)} %eq.39, pred[1152]{0:T(1024)(128)(4,1)S(1)} %and.37, ...), kind=kLoop, calls=%fused_computation.33 | loop fusion | flops 7518336 | bytes 8870016 | tf_op jit(solution)/shard_map/reduce_sum | solution.py:43
  45.9 1.6 fusion.15
  47.6 1.6 fusion.16
  49.2 1.6 fusion.17
  50.9 1.6 fusion.18
  52.5 1.6 fusion.19
  54.2 3.6 %collective-permute-start.7 = (bf16[640,1280]{1,0:T(8,128)(2,1)S(1)}, bf16[640,1280]{1,0:T(8,128)(2,1)}, u32[]{:S(2)}, u32[]{:S(2)}) collective-permute-start(bf16[640,1280]{1,0:T(8,128)(2,1)S(1)} %copy-done), channel_id=1, source_target_pairs={{0,12},{4,0},{8,4},{12,8},{1,13},{5,1},{9,5},{13,9},{2,14},{6,2},{... | collective-permute-start | bytes 4915208 | tf_op jit(solution)/shard_map/ppermute | solution.py:23
  57.8 23.6 %collective-permute-done.6 = bf16[640,1280]{1,0:T(8,128)(2,1)S(1)} collective-permute-done((bf16[640,1280]{1,0:T(8,128)(2,1)}, bf16[640,1280]{1,0:T(8,128)(2,1)S(1)}, u32[]{:S(2)}, u32[]{:S(2)}) %collective-permute-start.6) | collective-permute-done | bytes 1638432 | tf_op jit(solution)/shard_map/ppermute | solution.py:20
  81.4 3.2 %broadcast_in_dim.38 = bf16[2560,1280]{1,0:T(8,128)(2,1)} broadcast(bf16[]{:T(256)} %constant.50.clone.1), dimensions={} | broadcast | bytes 6553602 | tf_op jit(solution)/shard_map/broadcast_in_dim | solution.py:16
  84.6 1.3 constant_dynamic-update-slice_fusion.3
  85.9 1.3 constant_dynamic-update-slice_fusion.2
  87.2 29.4 %collective-permute-done.7 = bf16[640,1280]{1,0:T(8,128)(2,1)} collective-permute-done((bf16[640,1280]{1,0:T(8,128)(2,1)S(1)}, bf16[640,1280]{1,0:T(8,128)(2,1)}, u32[]{:S(2)}, u32[]{:S(2)}) %collective-permute-start.7) | collective-permute-done | bytes 1638432 | tf_op jit(solution)/shard_map/ppermute | solution.py:23
  116.6 2.7 %constant_dynamic-update-slice_fusion.1 = bf16[2560,1280]{1,0:T(8,128)(2,1)} fusion(bf16[2560,1280]{1,0:T(8,128)(2,1)} %constant_dynamic-update-slice_fusion.2, bf16[640,1280]{1,0:T(8,128)(2,1)} %collective-permute-done.7, s32[]{:T(128)S(6)} %select_n.77), kind=kLoop, calls=%fused_computation.63 | loop fusion | bytes 3276804 | tf_op jit(solution)/shard_map/dynamic_update_slice | solution.py:24
  119.3 30.4 %collective-permute-done.8 = bf16[640,1280]{1,0:T(8,128)(2,1)} collective-permute-done((bf16[640,1280]{1,0:T(8,128)(2,1)S(1)}, bf16[640,1280]{1,0:T(8,128)(2,1)}, u32[]{:S(2)}, u32[]{:S(2)}) %collective-permute-start.8) | collective-permute-done | bytes 1638432 | tf_op jit(solution)/shard_map/ppermute | solution.py:20
  149.7 2.7 %constant_dynamic-update-slice_fusion = bf16[2560,1280]{1,0:T(8,128)(2,1)} fusion(bf16[2560,1280]{1,0:T(8,128)(2,1)} %constant_dynamic-update-slice_fusion.1, bf16[640,1280]{1,0:T(8,128)(2,1)} %collective-permute-done.8, s32[]{:T(128)S(6)} %select_n.79), kind=kLoop, calls=%fused_computation.62 | loop fusion | bytes 3276804 | tf_op jit(solution)/shard_map/dynamic_update_slice | solution.py:21
  152.4 7.1 %convolution_convert_fusion = bf16[384,1280]{1,0:T(8,128)(2,1)} fusion(bf16[384,2560]{1,0:T(8,128)(2,1)} %all-gather.2.cloned.1.call-done, bf16[2560,1280]{1,0:T(8,128)(2,1)} %constant_dynamic-update-slice_fusion), kind=kOutput, calls=%fused_computation.15 | convolution fusion | flops 2517073920 | bytes 9502720 | tf_op jit(solution)/shard_map/dot_general | solution.py:104
  (27 shorter events, 3.5 us)
Async XLA Ops:
  6.5 28.4 %copy-start.2 = (s32[384]{0:T(512)S(1)}, s32[384]{0:T(512)}, u32[]{:S(2)}) copy-start(s32[384]{0:T(512)} %param.12) | copy-start | bytes 4612
  6.5 145.9 %all-gather.2.cloned.1.call-start = ((), (), s32[]{:S(2)}) async-start(), calls=%async_computation | async-start | bytes 2457600 | tf_op jit(solution)/shard_map/all_gather | solution.py:100
  6.5 19.8 %collective-permute-start = (s32[384]{0:T(512)}, s32[384]{0:T(512)S(1)}, u32[]{:S(2)}, u32[]{:S(2)}) collective-permute-start(s32[384]{0:T(512)} %param.12), channel_id=1, source_target_pairs={{0,4},{4,8},{8,12},{1,5},{5,9},{9,13},{2,6},{6,10},{10,14},{3,7},{... | collective-permute-start | bytes 4616 | tf_op jit(solution)/shard_map/ppermute | solution.py:33
  11.6 16.1 %collective-permute-start.1 = (s32[384]{0:T(512)}, s32[384]{0:T(512)S(1)}, u32[]{:S(2)}, u32[]{:S(2)}) collective-permute-start(s32[384]{0:T(512)} %param.12), channel_id=1, source_target_pairs={{4,0},{8,4},{12,8},{5,1},{9,5},{13,9},{6,2},{10,6},{14,10},{7,3},{... | collective-permute-start | bytes 4616 | tf_op jit(solution)/shard_map/ppermute | solution.py:33
  12.9 17.6 %collective-permute-start.2 = (bf16[384,640]{1,0:T(8,128)(2,1)}, bf16[384,640]{1,0:T(8,128)(2,1)S(1)}, u32[]{:S(2)}, u32[]{:S(2)}) collective-permute-start(bf16[384,640]{1,0:T(8,128)(2,1)} %param.8), channel_id=1, source_target_pairs={{0,4},{4,8},{8,12},{1,5},{5,9},{9,13},{2,6},{6,10},{10,14},{3,7},{... | collective-permute-start | bytes 1474568 | tf_op jit(solution)/shard_map/ppermute | solution.py:33
  17.5 16.3 %collective-permute-start.3 = (bf16[384,640]{1,0:T(8,128)(2,1)}, bf16[384,640]{1,0:T(8,128)(2,1)S(1)}, u32[]{:S(2)}, u32[]{:S(2)}) collective-permute-start(bf16[384,640]{1,0:T(8,128)(2,1)} %param.8), channel_id=1, source_target_pairs={{4,0},{8,4},{12,8},{5,1},{9,5},{13,9},{6,2},{10,6},{14,10},{7,3},{... | collective-permute-start | bytes 1474568 | tf_op jit(solution)/shard_map/ppermute | solution.py:33
  18.8 21.2 %collective-permute-start.4 = (bf16[384,640]{1,0:T(8,128)(2,1)}, bf16[384,640]{1,0:T(8,128)(2,1)S(1)}, u32[]{:S(2)}, u32[]{:S(2)}) collective-permute-start(bf16[384,640]{1,0:T(8,128)(2,1)} %param.9), channel_id=1, source_target_pairs={{0,4},{4,8},{8,12},{1,5},{5,9},{9,13},{2,6},{6,10},{10,14},{3,7},{... | collective-permute-start | bytes 1474568 | tf_op jit(solution)/shard_map/ppermute | solution.py:33
  26.4 16.0 %collective-permute-start.5 = (bf16[384,640]{1,0:T(8,128)(2,1)}, bf16[384,640]{1,0:T(8,128)(2,1)}, u32[]{:S(2)}, u32[]{:S(2)}) collective-permute-start(bf16[384,640]{1,0:T(8,128)(2,1)} %param.9), channel_id=1, source_target_pairs={{4,0},{8,4},{12,8},{5,1},{9,5},{13,9},{6,2},{10,6},{14,10},{7,3},{... | collective-permute-start | bytes 1474568 | tf_op jit(solution)/shard_map/ppermute | solution.py:33
  27.7 53.7 %collective-permute-start.6 = (bf16[640,1280]{1,0:T(8,128)(2,1)}, bf16[640,1280]{1,0:T(8,128)(2,1)S(1)}, u32[]{:S(2)}, u32[]{:S(2)}) collective-permute-start(bf16[640,1280]{1,0:T(8,128)(2,1)} %param.10), channel_id=1, source_target_pairs={{0,4},{4,8},{8,12},{12,0},{1,5},{5,9},{9,13},{13,1},{2,6},{6,10},{... | collective-permute-start | bytes 4915208 | tf_op jit(solution)/shard_map/ppermute | solution.py:20
  30.4 4.6 %copy-start.3 = (bf16[384,640]{1,0:T(8,128)(2,1)S(1)}, bf16[384,640]{1,0:T(8,128)(2,1)}, u32[]{:S(2)}) copy-start(bf16[384,640]{1,0:T(8,128)(2,1)} %param.7) | copy-start | bytes 1474564
  37.5 4.9 %copy-start.1 = (bf16[384,640]{1,0:T(8,128)(2,1)S(1)}, bf16[384,640]{1,0:T(8,128)(2,1)}, u32[]{:S(2)}) copy-start(bf16[384,640]{1,0:T(8,128)(2,1)} %param.9) | copy-start | bytes 1474564
  52.5 1.7 %copy-start = (bf16[640,1280]{1,0:T(8,128)(2,1)S(1)}, bf16[640,1280]{1,0:T(8,128)(2,1)}, u32[]{:S(2)}) copy-start(bf16[640,1280]{1,0:T(8,128)(2,1)} %param.10) | copy-start | bytes 4915204
  54.2 62.4 %collective-permute-start.7 = (bf16[640,1280]{1,0:T(8,128)(2,1)S(1)}, bf16[640,1280]{1,0:T(8,128)(2,1)}, u32[]{:S(2)}, u32[]{:S(2)}) collective-permute-start(bf16[640,1280]{1,0:T(8,128)(2,1)S(1)} %copy-done), channel_id=1, source_target_pairs={{0,12},{4,0},{8,4},{12,8},{1,13},{5,1},{9,5},{13,9},{2,14},{6,2},{... | collective-permute-start | bytes 4915208 | tf_op jit(solution)/shard_map/ppermute | solution.py:23
  81.4 68.3 %collective-permute-start.8 = (bf16[640,1280]{1,0:T(8,128)(2,1)S(1)}, bf16[640,1280]{1,0:T(8,128)(2,1)}, u32[]{:S(2)}, u32[]{:S(2)}) collective-permute-start(bf16[640,1280]{1,0:T(8,128)(2,1)S(1)} %collective-permute-done.6), channel_id=1, source_target_pairs={{0,4},{4,8},{8,12},{12,0},{1,5},{5,9},{9,13},{13,1},{2,6},{6,10},{... | collective-permute-start | bytes 4915208 | tf_op jit(solution)/shard_map/ppermute | solution.py:20
Sparse Core Ops, SparseCore 0:
  54.3 24.0 all-gather.1
